TPU v7x, 32 devices: a whole 2x2x4 slice. The times are simulated.
32 devices in a mesh: req: 8 (over y, x, core), tp: 4 (over z).
Axes of the slice: x: 2, y: 2, z: 4, core: 2. Of those that a mesh axis runs over, the one named last changes fastest.
Arguments:
- queries: bfloat16 [1536, 2560], P('req', 'tp'), may hold values from -5 to 5
- new_keys: bfloat16 [1536, 512], P('req', 'tp'), may hold values from -5 to 5
- new_values: bfloat16 [1536, 512], P('req', 'tp'), may hold values from -5 to 5
- key_pages: bfloat16 [512, 64, 512], P('req', None, 'tp'), may hold values from -5 to 5
- value_pages: bfloat16 [512, 64, 512], P('req', None, 'tp'), may hold values from -5 to 5
- page_table: int32 [32, 16], P('req'), may hold values from 0 to 511, as said below
- cache_lengths: int32 [32], P('req'), may hold values from 2 to 1024, as said below
- parents: int32 [32, 48], P('req'), may hold values from -1 to 46, as said below
- residual: bfloat16 [1536, 2560], P('req'), may hold values from -6 to 6
- out_weight: bfloat16 [2560, 2560], P('tp'), may hold values from -0.125 to 0.125
- norm_gain: float32 [2560], replicated, may hold values from 0.1 to 1.9
- router_weight: float32 [2560, 16], replicated, may hold values from -0.125 to 0.125
- routes: int32 [1536, 6], P('req'), may hold values from 0 to 15, all different within a row; in each aligned block of 192 rows (0 to 191, 192 to 383, ...) at most 91 rows name the same one
- expert_gate_up: bfloat16 [16, 2560, 2, 1536], P('req', None, None, 'tp'), may hold values from -0.125 to 0.125
- expert_down: bfloat16 [16, 1536, 2560], P('req', 'tp'), may hold values from -0.15625 to 0.15625
- shared_gate_up: bfloat16 [2560, 2, 1536], P(None, None, 'tp'), may hold values from -0.125 to 0.125
- shared_down: bfloat16 [1536, 2560], P('tp'), may hold values from -0.15625 to 0.15625
Outputs:
- layer_out: bfloat16 [1536, 2560], P('req', 'tp')
Inputs may be any that keep to these rules, and one draw needn't show every extreme that they name: `page_table`: the pages of the 4 requests of the d-th block of 4 rows are the d-th block of 64 pages of the pool, each named once. `cache_lengths`: some request holds 1024 positions. parents[r, 0] = -1, and 0 <= parents[r, i] < i for i >= 1. `routes`: A token's 6 experts differ. In each aligned block of 192 rows no expert is named by more than 91 rows, and in some block one expert is named by exactly 91.
All inputs are finite; a program needn't handle non-finite values.
Results may differ from a plain program's by a relative error of at most 0.02.
Values may be sent and summed in bfloat16 or wider, within the bound.
No kernel may reach another device: no remote copies, remote signals or barrier semaphores. Data moves between devices by JAX's collectives and lax.ppermute only.
A program may use at most 128 MiB of HBM per device.

v0:
```python
import math
import jax
import jax.numpy as jnp
from jax import lax
from jax.sharding import PartitionSpec as P

QH = 20
KVH = 4
HD = 128
EPSILON = 1e-06
NEGATIVE = -1e30


def rounded(values):
    return lax.optimization_barrier(values.astype(jnp.bfloat16)).astype(jnp.float32)


def ancestors(parents):
    tree_size = parents.shape[-1]
    position = jnp.arange(tree_size, dtype=jnp.int32)
    adjacency = (parents[..., :, None] == position[None, :]) | (
        position[:, None] == position[None, :]
    )
    closure = adjacency.astype(jnp.float32)
    for doubling in range(max(1, (tree_size - 1).bit_length())):
        closure = jnp.minimum(
            jnp.einsum("...ij,...jk->...ik", closure, closure, precision=lax.Precision.HIGHEST), 1.0
        )
    return closure > 0.5


def tree_attention(queries, cache_keys, cache_values, new_keys, new_values, lengths, allowed):
    scaling = 1.0 / math.sqrt(queries.shape[-1])
    cache_scores = (
        jnp.einsum("rtkgd,rckd->rkgtc", queries, cache_keys, preferred_element_type=jnp.float32)
        * scaling
    )
    tree_scores = (
        jnp.einsum("rtkgd,rskd->rkgts", queries, new_keys, preferred_element_type=jnp.float32)
        * scaling
    )
    live = jnp.arange(cache_keys.shape[1], dtype=jnp.int32)[None, :] < lengths[:, None]
    cache_scores = jnp.where(live[:, None, None, None, :], cache_scores, NEGATIVE)
    tree_scores = jnp.where(allowed[:, None, None, :, :], tree_scores, NEGATIVE)
    highest = jnp.maximum(jnp.max(cache_scores, axis=-1), jnp.max(tree_scores, axis=-1))[..., None]
    cache_exp = jnp.exp(cache_scores - highest)
    tree_exp = jnp.exp(tree_scores - highest)
    denominator = (jnp.sum(cache_exp, axis=-1) + jnp.sum(tree_exp, axis=-1))[..., None]
    cache_probs = (cache_exp / denominator).astype(jnp.bfloat16)
    tree_probs = (tree_exp / denominator).astype(jnp.bfloat16)
    mixed = jnp.einsum(
        "rkgtc,rckd->rtkgd", cache_probs, cache_values, preferred_element_type=jnp.float32
    )
    mixed = mixed + jnp.einsum(
        "rkgts,rskd->rtkgd", tree_probs, new_values, preferred_element_type=jnp.float32
    )
    return mixed.astype(jnp.bfloat16).reshape(queries.shape[0], queries.shape[1], -1)


def shards(
    queries,
    new_keys,
    new_values,
    key_pages,
    value_pages,
    page_table,
    cache_lengths,
    parents,
    residual,
    out_weight,
    norm_gain,
    router_weight,
    routes,
    expert_gate_up,
    expert_down,
    shared_gate_up,
    shared_down,
):
    groups = lax.axis_size("req")
    tp_count = lax.axis_size("tp")
    requests = parents.shape[0]
    tree_size = parents.shape[1]
    row_count = requests * tree_size
    kv_local = new_keys.shape[1] // HD
    head_ratio = QH // KVH
    model_width = residual.shape[1]
    part_width = model_width // tp_count
    pages_dev = key_pages.shape[0]
    local_pages = page_table - lax.axis_index("req") * pages_dev
    cache_keys = key_pages[local_pages].reshape(requests, -1, kv_local, HD)
    cache_values = value_pages[local_pages].reshape(requests, -1, kv_local, HD)
    head_outputs = tree_attention(
        queries.reshape(requests, tree_size, kv_local, head_ratio, HD),
        cache_keys,
        cache_values,
        new_keys.reshape(requests, tree_size, kv_local, HD),
        new_values.reshape(requests, tree_size, kv_local, HD),
        cache_lengths,
        ancestors(parents),
    )
    attn_terms = jnp.dot(
        head_outputs.reshape(row_count, -1), out_weight, preferred_element_type=jnp.float32
    )
    column = lax.axis_index("tp") * part_width
    experts_local = expert_gate_up.shape[0]
    top_count = routes.shape[1]
    expert_count = experts_local * groups
    capacity = max(10 * requests, row_count * top_count * 5 // (4 * expert_count) + 1)
    capacity = -(-capacity // 16) * 16
    slot_count = expert_count * capacity
    flat_expert = routes.reshape(-1)
    expert_ids = jnp.arange(expert_count, dtype=jnp.int32)
    onehot = (flat_expert[:, None] == expert_ids[None, :]).astype(jnp.int32)
    earlier = jnp.cumsum(onehot, axis=0) - onehot
    rank = jnp.sum(earlier * onehot, axis=1)
    slot = (flat_expert * capacity + rank).reshape(row_count, top_count)
    slot_ids = jnp.arange(slot_count, dtype=jnp.int32)
    hit = slot[:, :, None] == slot_ids[None, None, :]
    attn_blocks = attn_terms.astype(jnp.bfloat16).reshape(row_count, tp_count, part_width)
    attn_blocks = lax.all_to_all(
        attn_blocks.transpose(1, 0, 2), "tp", split_axis=0, concat_axis=0, tiled=True
    )
    attn_part = jnp.sum(attn_blocks.astype(jnp.float32), axis=0)
    residual_part = lax.dynamic_slice_in_dim(residual, column, part_width, 1)
    hidden_part_bf = (residual_part.astype(jnp.float32) + attn_part).astype(jnp.bfloat16)
    hidden_bf = lax.all_gather(hidden_part_bf[None], "tp", axis=0, tiled=True)
    hidden = hidden_bf.transpose(1, 0, 2).reshape(row_count, model_width).astype(jnp.float32)
    rstd = lax.rsqrt(jnp.mean(hidden * hidden, axis=1, keepdims=True) + EPSILON)
    normed = hidden * rstd * norm_gain
    logits = jnp.dot(normed, router_weight, precision=lax.Precision.HIGHEST)
    normed_bf = normed.astype(jnp.bfloat16)
    hidden_part = hidden_part_bf.astype(jnp.float32)
    near_width = part_width // 2
    far_width = part_width - near_width
    normed_blocks = normed_bf.reshape(row_count, tp_count, part_width)
    normed_near = normed_blocks[:, :, :near_width].reshape(row_count, tp_count * near_width)
    normed_far = lax.dynamic_slice_in_dim(normed_bf, column + near_width, far_width, 1)
    send_rows = jnp.concatenate([normed_near, normed_far], axis=1)
    dispatch = jnp.any(hit, axis=1).astype(jnp.bfloat16)
    dispatch = dispatch.reshape(row_count, groups, experts_local, capacity)
    returns = []
    for expert in range(experts_local):
        outbox = jnp.einsum(
            "tgc,tk->gck", dispatch[:, :, expert], send_rows, preferred_element_type=jnp.float32
        ).astype(jnp.bfloat16)
        arrived = lax.all_to_all(outbox, "req", split_axis=0, concat_axis=0, tiled=True)
        arrived = arrived.reshape(groups * capacity, -1)
        rows_near = arrived[:, : tp_count * near_width]
        rows_far = lax.all_gather(
            arrived[None, :, tp_count * near_width :], "tp", axis=0, tiled=True
        )
        weight_blocks = expert_gate_up[expert].reshape(tp_count, part_width, 2, -1)
        weight_near = weight_blocks[:, :near_width].reshape(tp_count * near_width, 2, -1)
        weight_far = weight_blocks[:, near_width:]
        gate_up = jnp.einsum(
            "mk,kcf->mcf", rows_near, weight_near, preferred_element_type=jnp.float32
        ) + jnp.einsum("zmk,zkcf->mcf", rows_far, weight_far, preferred_element_type=jnp.float32)
        act = (jax.nn.silu(gate_up[:, 0]) * gate_up[:, 1]).astype(jnp.bfloat16)
        partial_value = jnp.dot(act, expert_down[expert], preferred_element_type=jnp.float32)
        partial_blocks = partial_value.astype(jnp.bfloat16).reshape(-1, tp_count, part_width)
        back_near = partial_blocks[:, :, :near_width].reshape(-1, tp_count * near_width)
        far_parts = lax.all_to_all(
            partial_blocks[:, :, near_width:].transpose(1, 0, 2),
            "tp",
            split_axis=0,
            concat_axis=0,
            tiled=True,
        )
        back_far = jnp.sum(far_parts.astype(jnp.float32), axis=0).astype(jnp.bfloat16)
        outputs = jnp.concatenate([back_near, back_far], axis=1).reshape(groups, capacity, -1)
        returns.append(lax.all_to_all(outputs, "req", split_axis=0, concat_axis=0, tiled=True))
    chosen = jnp.sum(
        jnp.where(routes[:, :, None] == expert_ids[None, None, :], logits[:, None, :], 0.0), axis=-1
    )
    gate_values = jax.nn.sigmoid(chosen)
    gate_values = gate_values / jnp.sum(gate_values, axis=1, keepdims=True)
    weights = jnp.sum(jnp.where(hit, gate_values[:, :, None], 0.0), axis=1)
    weights = weights.reshape(row_count, groups, experts_local, capacity)
    weights_hi = weights.astype(jnp.bfloat16)
    weights_lo = (weights - weights_hi.astype(jnp.float32)).astype(jnp.bfloat16)
    routed = jnp.zeros((row_count, tp_count * near_width + far_width), jnp.float32)
    for expert in range(experts_local):
        for split in (weights_hi, weights_lo):
            routed = routed + jnp.einsum(
                "tgc,gck->tk",
                split[:, :, expert],
                returns[expert],
                preferred_element_type=jnp.float32,
            )
    routed_near = routed[:, : tp_count * near_width].reshape(row_count, tp_count, near_width)
    routed_far = routed[:, tp_count * near_width :]
    shared_gu = jnp.einsum(
        "td,dcf->tcf", normed_bf, shared_gate_up, preferred_element_type=jnp.float32
    )
    shared_act = (jax.nn.silu(shared_gu[:, 0]) * shared_gu[:, 1]).astype(jnp.bfloat16)
    shared_terms = jnp.dot(shared_act, shared_down, preferred_element_type=jnp.float32)
    shared_blocks = shared_terms.reshape(row_count, tp_count, part_width)
    total = jnp.concatenate(
        [shared_blocks[:, :, :near_width] + routed_near, shared_blocks[:, :, near_width:]], axis=2
    ).astype(jnp.bfloat16)
    total = lax.all_to_all(total.transpose(1, 0, 2), "tp", split_axis=0, concat_axis=0, tiled=True)
    summed = jnp.sum(total.astype(jnp.float32), axis=0)
    summed = summed + jnp.concatenate(
        [jnp.zeros((row_count, near_width), jnp.float32), routed_far], axis=1
    )
    return (hidden_part + summed).astype(jnp.bfloat16)


def solution(mesh):
    in_specs = (
        P("req", "tp"),
        P("req", "tp"),
        P("req", "tp"),
        P("req", None, "tp"),
        P("req", None, "tp"),
        P("req", None),
        P("req"),
        P("req", None),
        P("req", None),
        P("tp", None),
        P(),
        P(),
        P("req", None),
        P("req", None, None, "tp"),
        P("req", "tp", None),
        P(None, None, "tp"),
        P("tp", None),
    )
    out_specs = P("req", "tp")
    return jax.shard_map(shards, mesh=mesh, in_specs=in_specs, out_specs=out_specs, check_vma=False)
```

profile of v0, /device:TPU:2, one launch (start us, length us, event | category | flops | bytes accessed | tf_op | source)
XLA Modules:
  0.0 446.8 jit_solution(14865229061335307913)
XLA Ops:
  28.5 4.9 %all-to-all-start = ((bf16[4,192,640]{2,1,0:T(8,128)(2,1)}), bf16[4,192,640]{2,1,0:T(8,128)(2,1)S(1)}, u32[]{:S(2)}, u32[]{:S(2)}) async-start(bf16[4,192,640]{2,1,0:T(8,128)(2,1)} %bitcast.226), calls=%async_computation | async-start | bytes 1966080 | tf_op jit(solution)/shard_map/all_to_all | solution.py:120
  33.8 4.5 %reduce-window.6 = s32[16,9,128]{2,1,0:T(8,128)S(1)} reduce-window(s32[16,9,128]{2,1,0:T(8,128)S(1)} %fusion.52, s32[]{:T(128)} %constant.20.clone.1), window={size=1x1x128 pad=0_0x0_0x127_0}, to_apply=%region_6.7 | reduce-window | flops 2340864 | bytes 147460 | tf_op jit(solution)/shard_map/reduce-window
  41.8 15.9 %all-to-all-done = bf16[4,192,640]{2,1,0:T(8,128)(2,1)S(1)} async-done(((bf16[4,192,640]{2,1,0:T(8,128)(2,1)}), bf16[4,192,640]{2,1,0:T(8,128)(2,1)S(1)}, u32[]{:S(2)}, u32[]{:S(2)}) %all-to-all-start) | async-done | bytes 983072 | tf_op jit(solution)/shard_map/all_to_all | solution.py:120
  58.8 19.7 %all-gather = bf16[768,640]{1,0:T(8,128)(2,1)S(1)} all-gather(bf16[192,640]{1,0:T(8,128)(2,1)S(1)} %add_convert_fusion.1), channel_id=2, replica_groups=mesh['req'=8,'tp'=4] {'tp'}, dimensions={0}, use_global_device_ids=true | all-gather | bytes 1228800 | tf_op jit(solution)/shard_map/all_gather | solution.py:126
  86.8 34.1 %all_to_all.40 = bf16[8,96,1600]{2,1,0:T(8,128)(2,1)S(1)} all-to-all(bf16[8,96,1600]{2,1,0:T(8,128)(2,1)S(1)} %convolution_convert_fusion.4), channel_id=1, replica_groups=mesh['req'=8,'tp'=4] {'req'}, dimensions={0} | all-to-all | bytes 4915200 | tf_op jit(solution)/shard_map/all_to_all | solution.py:146
  125.7 5.7 %all-to-all-start.4 = ((bf16[8,96,1600]{2,1,0:T(8,128)(2,1)}), bf16[8,96,1600]{2,1,0:T(8,128)(2,1)}, u32[]{:S(2)}, u32[]{:S(2)}) async-start(bf16[8,96,1600]{2,1,0:T(8,128)(2,1)} %convolution_convert_fusion.3), calls=%async_computation.4 | async-start | bytes 5111808 | tf_op jit(solution)/shard_map/all_to_all | solution.py:146
  131.7 7.6 %fusion.67 = (bf16[1,2560,2,384]{3,2,1,0:T(2,128)(2,1)S(1)}, bf16[1,2560,2,384]{3,2,1,0:T(2,128)(2,1)}) fusion(bf16[2,2560,2,384]{3,2,1,0:T(2,128)(2,1)} %param.30), kind=kLoop, calls=%fused_computation.137 | loop fusion | bytes 15728640 | tf_op jit(solution)/shard_map/slice | solution.py:152
  143.2 18.4 %all-to-all-done.4 = bf16[8,96,1600]{2,1,0:T(8,128)(2,1)} async-done(((bf16[8,96,1600]{2,1,0:T(8,128)(2,1)}), bf16[8,96,1600]{2,1,0:T(8,128)(2,1)}, u32[]{:S(2)}, u32[]{:S(2)}) %all-to-all-start.4) | async-done | bytes 2457632 | tf_op jit(solution)/shard_map/all_to_all | solution.py:146
  163.6 9.5 %all-gather.6.cloned.1.call-done = bf16[3072,320]{1,0:T(8,128)(2,1)} async-done(((bf16[768,320]{1,0:T(8,128)(2,1)}), bf16[3072,320]{1,0:T(8,128)(2,1)}) %all-gather.6.cloned.1.call-update) | async-done | bytes 1966096 | tf_op jit(solution)/shard_map/all_gather | solution.py:149
  173.2 4.1 fusion.11
  179.5 4.2 convolution_convert_fusion.1
  183.7 7.6 %reshape.244 = bf16[768,4,640]{2,1,0:T(4,128)(2,1)} reshape(bf16[768,2560]{1,0:T(8,128)(2,1)} %convolution_convert_fusion.1) | data formatting | bytes 7864320 | tf_op jit(solution)/shard_map/reshape | solution.py:160
  191.3 7.4 %fusion.68 = (bf16[768,4,320]{2,1,0:T(4,128)(2,1)}, bf16[768,4,320]{2,1,0:T(4,128)(2,1)}) fusion(bf16[768,4,640]{2,1,0:T(4,128)(2,1)} %reshape.244), kind=kLoop, calls=%fused_computation.138 | loop fusion | bytes 7864320 | tf_op jit(solution)/shard_map/slice | solution.py:161
  198.7 5.4 %copy.182 = bf16[768,4,320]{0,2,1:T(8,128)(2,1)} copy(bf16[768,4,320]{2,1,0:T(4,128)(2,1)} %get-tuple-element.8) | data formatting | bytes 3932160
  204.0 4.8 %all-to-all-start.2 = ((bf16[4,768,320]{1,2,0:T(8,128)(2,1)}), bf16[4,768,320]{1,2,0:T(8,128)(2,1)}, u32[]{:S(2)}, u32[]{:S(2)}) async-start(bf16[4,768,320]{1,2,0:T(8,128)(2,1)} %bitcast.238), calls=%async_computation.2 | async-start | bytes 3932160 | tf_op jit(solution)/shard_map/all_to_all | solution.py:162
  214.9 25.5 %all-gather.8.cloned.1.call-done = bf16[3072,320]{1,0:T(8,128)(2,1)} async-done(((bf16[768,320]{1,0:T(8,128)(2,1)}), bf16[3072,320]{1,0:T(8,128)(2,1)}) %all-gather.8.cloned.1.call-update) | async-done | bytes 1966096 | tf_op jit(solution)/shard_map/all_gather | solution.py:149
  240.4 4.1 fusion.8
  248.0 4.1 convolution_convert_fusion
  252.1 7.6 %reshape.247 = bf16[768,4,640]{2,1,0:T(4,128)(2,1)} reshape(bf16[768,2560]{1,0:T(8,128)(2,1)} %convolution_convert_fusion) | data formatting | bytes 7864320 | tf_op jit(solution)/shard_map/reshape | solution.py:160
  259.7 7.3 %fusion.69 = (bf16[768,4,320]{2,1,0:T(4,128)(2,1)}, bf16[768,4,320]{2,1,0:T(4,128)(2,1)}) fusion(bf16[768,4,640]{2,1,0:T(4,128)(2,1)} %reshape.247), kind=kLoop, calls=%fused_computation.139 | loop fusion | bytes 7864320 | tf_op jit(solution)/shard_map/slice | solution.py:161
  267.0 5.3 %copy.184 = bf16[768,4,320]{0,2,1:T(8,128)(2,1)} copy(bf16[768,4,320]{2,1,0:T(4,128)(2,1)} %get-tuple-element.10) | data formatting | bytes 3932160
  272.3 4.4 all-to-all-start.5
  276.8 4.7 %concatenate.27 = bf16[8,96,1280]{2,1,0:T(8,128)(2,1)} reshape(bf16[768,4,320]{2,1,0:T(4,128)(2,1)} %get-tuple-element.7) | data formatting | bytes 3932160 | tf_op jit(solution)/shard_map/concatenate | solution.py:170
  287.1 34.9 %all-to-all-done.5 = bf16[4,768,320]{1,2,0:T(8,128)(2,1)} async-done(((bf16[4,768,320]{1,2,0:T(8,128)(2,1)}), bf16[4,768,320]{1,2,0:T(8,128)(2,1)}, u32[]{:S(2)}, u32[]{:S(2)}) %all-to-all-start.5) | async-done | bytes 1966112 | tf_op jit(solution)/shard_map/all_to_all | solution.py:162
  322.0 4.8 %all-to-all-start.3 = ((bf16[8,96,1600]{2,1,0:T(8,128)(2,1)}), bf16[8,96,1600]{2,1,0:T(8,128)(2,1)}, u32[]{:S(2)}, u32[]{:S(2)}) async-start(bf16[8,96,1600]{2,1,0:T(8,128)(2,1)} %pad_maximum_fusion), calls=%async_computation.3 | async-start | bytes 5111808 | tf_op jit(solution)/shard_map/all_to_all | solution.py:171
  326.8 4.1 copy.178
  330.9 4.7 %concatenate.30 = bf16[8,96,1280]{2,1,0:T(8,128)(2,1)} reshape(bf16[768,4,320]{2,1,0:T(4,128)(2,1)} %get-tuple-element.9) | data formatting | bytes 3932160 | tf_op jit(solution)/shard_map/concatenate | solution.py:170
  341.2 15.8 %all-to-all-done.3 = bf16[8,96,1600]{2,1,0:T(8,128)(2,1)} async-done(((bf16[8,96,1600]{2,1,0:T(8,128)(2,1)}), bf16[8,96,1600]{2,1,0:T(8,128)(2,1)}, u32[]{:S(2)}, u32[]{:S(2)}) %all-to-all-start.3) | async-done | bytes 2457632 | tf_op jit(solution)/shard_map/all_to_all | solution.py:171
  357.0 6.0 %all-to-all-start.6 = ((bf16[8,96,1600]{2,1,0:T(8,128)(2,1)}), bf16[8,96,1600]{2,1,0:T(8,128)(2,1)}, u32[]{:S(2)}, u32[]{:S(2)}) async-start(bf16[8,96,1600]{2,1,0:T(8,128)(2,1)} %pad_maximum_fusion.1), calls=%async_computation.6 | async-start | bytes 5111808 | tf_op jit(solution)/shard_map/all_to_all | solution.py:171
  377.9 15.3 %all-to-all-done.6 = bf16[8,96,1600]{2,1,0:T(8,128)(2,1)} async-done(((bf16[8,96,1600]{2,1,0:T(8,128)(2,1)}), bf16[8,96,1600]{2,1,0:T(8,128)(2,1)}, u32[]{:S(2)}, u32[]{:S(2)}) %all-to-all-start.6) | async-done | bytes 2457632 | tf_op jit(solution)/shard_map/all_to_all | solution.py:171
  407.4 4.4 all-to-all-start.7
  413.4 23.2 %all-to-all-done.7 = bf16[4,192,640]{2,1,0:T(8,128)(2,1)} async-done(((bf16[4,192,640]{2,1,0:T(8,128)(2,1)}), bf16[4,192,640]{2,1,0:T(8,128)(2,1)}, u32[]{:S(2)}, u32[]{:S(2)}) %all-to-all-start.7) | async-done | bytes 983072 | tf_op jit(solution)/shard_map/all_to_all | solution.py:201
  (149 shorter events, 102.3 us)
Async XLA Ops:
  6.5 19.9 %copy-start = (bf16[640,2560]{1,0:T(8,128)(2,1)S(1)}, bf16[640,2560]{1,0:T(8,128)(2,1)}, u32[]{:S(2)}) copy-start(bf16[640,2560]{1,0:T(8,128)(2,1)} %param.26) | copy-start | bytes 9830404
  15.4 2.2 copy-start.12
  15.4 2.2 copy-start.23
  17.5 1.9 copy-start.2
  18.0 1.6 copy-start.13
  22.5 3.5 copy-start.14
  22.5 3.5 copy-start.26
  27.4 5.9 %copy-start.22 = (s32[192,6]{0,1:T(8,128)S(1)}, s32[192,6]{0,1:T(8,128)}, u32[]{:S(2)}) copy-start(s32[192,6]{0,1:T(8,128)} %param.29) | copy-start | bytes 13828
  27.4 6.3 %copy-start.21 = (f32[2560]{0:T(1024)S(1)}, f32[2560]{0:T(1024)}, u32[]{:S(2)}) copy-start(f32[2560]{0:T(1024)} %param.27) | copy-start | bytes 30724
  28.5 29.2 %all-to-all-start = ((bf16[4,192,640]{2,1,0:T(8,128)(2,1)}), bf16[4,192,640]{2,1,0:T(8,128)(2,1)S(1)}, u32[]{:S(2)}, u32[]{:S(2)}) async-start(bf16[4,192,640]{2,1,0:T(8,128)(2,1)} %bitcast.226), calls=%async_computation | async-start | bytes 1966080 | tf_op jit(solution)/shard_map/all_to_all | solution.py:120
  33.4 139.8 %all-gather.6.cloned.1.call-start = ((), (), s32[]{:S(2)}) async-start(), calls=%async_computation.8 | async-start | bytes 2949120 | tf_op jit(solution)/shard_map/all_gather | solution.py:149
  120.9 1.5 copy-start.9
  125.7 35.9 %all-to-all-start.4 = ((bf16[8,96,1600]{2,1,0:T(8,128)(2,1)}), bf16[8,96,1600]{2,1,0:T(8,128)(2,1)}, u32[]{:S(2)}, u32[]{:S(2)}) async-start(bf16[8,96,1600]{2,1,0:T(8,128)(2,1)} %convolution_convert_fusion.3), calls=%async_computation.4 | async-start | bytes 5111808 | tf_op jit(solution)/shard_map/all_to_all | solution.py:146
  131.5 108.9 %all-gather.8.cloned.1.call-start = ((), (), s32[]{:S(2)}) async-start(), calls=%async_computation.9 | async-start | bytes 2949120 | tf_op jit(solution)/shard_map/all_gather | solution.py:149
  139.8 1.9 copy-start.3
  173.2 4.2 copy-start.10
  173.2 4.2 copy-start.15
  177.3 2.1 copy-start.24
  204.0 68.3 %all-to-all-start.2 = ((bf16[4,768,320]{1,2,0:T(8,128)(2,1)}), bf16[4,768,320]{1,2,0:T(8,128)(2,1)}, u32[]{:S(2)}, u32[]{:S(2)}) async-start(bf16[4,768,320]{1,2,0:T(8,128)(2,1)} %bitcast.238), calls=%async_computation.2 | async-start | bytes 3932160 | tf_op jit(solution)/shard_map/all_to_all | solution.py:162
  211.5 1.9 copy-start.4
  240.4 4.1 copy-start.16
  244.5 3.5 copy-start.25
  272.3 49.7 %all-to-all-start.5 = ((bf16[4,768,320]{1,2,0:T(8,128)(2,1)}), bf16[4,768,320]{1,2,0:T(8,128)(2,1)}, u32[]{:S(2)}, u32[]{:S(2)}) async-start(bf16[4,768,320]{1,2,0:T(8,128)(2,1)} %bitcast.239), calls=%async_computation.5 | async-start | bytes 3932160 | tf_op jit(solution)/shard_map/all_to_all | solution.py:162
  322.0 35.0 %all-to-all-start.3 = ((bf16[8,96,1600]{2,1,0:T(8,128)(2,1)}), bf16[8,96,1600]{2,1,0:T(8,128)(2,1)}, u32[]{:S(2)}, u32[]{:S(2)}) async-start(bf16[8,96,1600]{2,1,0:T(8,128)(2,1)} %pad_maximum_fusion), calls=%async_computation.3 | async-start | bytes 5111808 | tf_op jit(solution)/shard_map/all_to_all | solution.py:171
  341.2 21.8 %copy-start.20 = (f32[2560,16]{0,1:T(8,128)S(1)}, f32[2560,16]{0,1:T(8,128)}, u32[]{:S(2)}) copy-start(f32[2560,16]{0,1:T(8,128)} %param.28) | copy-start | bytes 491524
  357.0 36.2 %all-to-all-start.6 = ((bf16[8,96,1600]{2,1,0:T(8,128)(2,1)}), bf16[8,96,1600]{2,1,0:T(8,128)(2,1)}, u32[]{:S(2)}, u32[]{:S(2)}) async-start(bf16[8,96,1600]{2,1,0:T(8,128)(2,1)} %pad_maximum_fusion.1), calls=%async_computation.6 | async-start | bytes 5111808 | tf_op jit(solution)/shard_map/all_to_all | solution.py:171
  368.9 26.7 %copy-start.17 = (bf16[192,8,2,96]{3,0,1,2:T(8,128)(2,1)}, bf16[192,8,2,96]{3,0,1,2:T(8,128)(2,1)S(1)}, u32[]{:S(2)}) copy-start(bf16[192,8,2,96]{3,0,1,2:T(8,128)(2,1)S(1)} %copy.207) | copy-start | bytes 1769476
  368.9 3.7 copy-start.5
  373.5 1.9 copy-start.6
  401.9 3.1 copy-start.7
  406.0 33.8 %copy-start.1 = (bf16[640,2560]{1,0:T(8,128)(2,1)S(1)}, bf16[640,2560]{1,0:T(8,128)(2,1)}, u32[]{:S(2)}) copy-start(bf16[640,2560]{1,0:T(8,128)(2,1)} %param.26) | copy-start | bytes 9830404
  407.4 29.3 %all-to-all-start.7 = ((bf16[4,192,640]{2,1,0:T(8,128)(2,1)}), bf16[4,192,640]{2,1,0:T(8,128)(2,1)}, u32[]{:S(2)}, u32[]{:S(2)}) async-start(bf16[4,192,640]{2,1,0:T(8,128)(2,1)} %maximum_bitcast_fusion), calls=%async_computation.7 | async-start | bytes 1966080 | tf_op jit(solution)/shard_map/all_to_all | solution.py:201
  (4 other events, 4.3 us)
Sparse Core Ops, SparseCore 0:
  123.5 49.6 all-gather.5
  174.7 65.5 all-gather.7
where the time goes:
time: 455 us; the launch traced here: 447 us
  waiting for transfers between devices  158 us (35%)
  local copies, waits for them, and re-layouts  105 us (23%)
  blocking collectives  53.8 us (12%)
  matrix products  50.7 us (11%)
  starting transfers between devices  35.3 us (8%)
  other arithmetic  28.9 us (6%)
  between operations  14.3 us (3%)
    all_gather x2, waiting for transfers between devices, shards(): lax.all_gather(arrived[None, :, tp_count * near_width:], 'tp', axis=0, ti...  35 us
    all_to_all x2, waiting for transfers between devices, shards(): lax.all_to_all(partial_blocks[:, :, near_width:].transpose(1, 0, 2), 'tp'...  34.9 us
    all_to_all x1, blocking collectives, shards(): lax.all_to_all(outbox, 'req', split_axis=0, concat_axis=0, tiled=True)  34.1 us
    all_to_all x2, waiting for transfers between devices, shards(): lax.all_to_all(outputs, 'req', split_axis=0, concat_axis=0, tiled=True)  31 us
    all_to_all x1, waiting for transfers between devices, shards(): lax.all_to_all(total.transpose(1, 0, 2), 'tp', split_axis=0, concat_axis=...  23.2 us
    unnamed x58, local copies, waits for them, and re-layouts  21.6 us
    all_gather x1, blocking collectives, shards(): hidden_bf = lax.all_gather(hidden_part_bf[None], 'tp', axis=0, tiled=True)  19.7 us
    all_to_all x1, waiting for transfers between devices, shards(): lax.all_to_all(outbox, 'req', split_axis=0, concat_axis=0, tiled=True)  18.4 us
  transfers between devices with their start and end apart: 9, of which 8 were waited for; matrix products, arithmetic and copies ran while one was open for 29% of the time, Pallas kernels for 0%

commit v1 on v0

--- a/solution.py
+++ b/solution.py
@@ -3,12 +3,25 @@
 import jax.numpy as jnp
 from jax import lax
 from jax.sharding import PartitionSpec as P
+from jax.lax import axis_index, axis_size, ppermute
 
 QH = 20
 KVH = 4
 HD = 128
 EPSILON = 1e-06
 NEGATIVE = -1e30
+
+
+def terms_show(u_in, mesh_ax):
+    main, row_out = (axis_size(mesh_ax), axis_index(mesh_ax))
+    extra, b_now = (u_in, 1)
+    while b_now < main:
+        q_next = ppermute(extra, mesh_ax, [(c, c ^ b_now) for c in range(main)])
+        odd = jnp.concatenate([extra, q_next], axis=0)
+        heard = jnp.concatenate([q_next, extra], axis=0)
+        extra = jnp.where(row_out & b_now == 0, odd, heard)
+        b_now = 2 * b_now
+    return extra
 
 
 def rounded(values):
@@ -146,9 +159,7 @@
         arrived = lax.all_to_all(outbox, "req", split_axis=0, concat_axis=0, tiled=True)
         arrived = arrived.reshape(groups * capacity, -1)
         rows_near = arrived[:, : tp_count * near_width]
-        rows_far = lax.all_gather(
-            arrived[None, :, tp_count * near_width :], "tp", axis=0, tiled=True
-        )
+        rows_far = terms_show(arrived[None, :, tp_count * near_width :], mesh_ax="tp")
         weight_blocks = expert_gate_up[expert].reshape(tp_count, part_width, 2, -1)
         weight_near = weight_blocks[:, :near_width].reshape(tp_count * near_width, 2, -1)
         weight_far = weight_blocks[:, near_width:]

time: 455 us -> 516 us (1.13)
  waiting for transfers between devices: 158 us -> 235 us
  blocking collectives: 53.8 us -> 19.7 us
  between operations: 14.3 us -> 0.83 us
  matrix products: 50.7 us -> 62.6 us
  starting transfers between devices: 35.3 us -> 47.1 us
    ppermute x0 -> x4, waiting for transfers between devices: none -> 108 us  [terms_show(): q_next = ppermute(extra, mesh_ax, [(c, c ^ b_now) for c in range(main)])]
    all_gather x2 -> x0, waiting for transfers between devices: 35 us -> none  [shards(): lax.all_gather(arrived[None, :, tp_count * near_width:], 'tp', axis=0, ti...]
    all_to_all x1 -> x0, blocking collectives: 34.1 us -> none  [shards(): lax.all_to_all(outbox, 'req', split_axis=0, concat_axis=0, tiled=True)]
    all_to_all x1 -> x2, waiting for transfers between devices: 18.4 us -> 27.8 us  [shards(): lax.all_to_all(outbox, 'req', split_axis=0, concat_axis=0, tiled=True)]
    ppermute x0 -> x4, local copies, waits for them, and re-layouts: none -> 7.42 us  [terms_show(): q_next = ppermute(extra, mesh_ax, [(c, c ^ b_now) for c in range(main)])]
    unnamed x58, local copies, waits for them, and re-layouts: 21.6 us -> 15 us
    ppermute x0 -> x4, starting transfers between devices: none -> 6.43 us  [terms_show(): q_next = ppermute(extra, mesh_ax, [(c, c ^ b_now) for c in range(main)])]
    all_to_all x2, waiting for transfers between devices: 31 us -> 24.7 us  [shards(): lax.all_to_all(outputs, 'req', split_axis=0, concat_axis=0, tiled=True)]
  transfers between devices with their start and end apart: 9 -> 12, of which waited for: 8 -> 9; matrix products, arithmetic and copies ran while one was open for 29% -> 31% of each run, Pallas kernels for 0% -> 0%
where the time goes in v1:
time: 516 us; the launch traced here: 507 us
  waiting for transfers between devices  235 us (46%)
  local copies, waits for them, and re-layouts  110 us (21%)
  matrix products  62.6 us (12%)
  starting transfers between devices  47.1 us (9%)
  other arithmetic  32.7 us (6%)
  blocking collectives  19.7 us (4%)
    ppermute x4, waiting for transfers between devices, terms_show(): q_next = ppermute(extra, mesh_ax, [(c, c ^ b_now) for c in range(main)])  108 us
    all_to_all x2, waiting for transfers between devices, shards(): lax.all_to_all(partial_blocks[:, :, near_width:].transpose(1, 0, 2), 'tp'...  34.7 us
    all_to_all x2, waiting for transfers between devices, shards(): lax.all_to_all(outbox, 'req', split_axis=0, concat_axis=0, tiled=True)  27.8 us
    all_to_all x2, waiting for transfers between devices, shards(): lax.all_to_all(outputs, 'req', split_axis=0, concat_axis=0, tiled=True)  24.7 us
    all_to_all x1, waiting for transfers between devices, shards(): lax.all_to_all(total.transpose(1, 0, 2), 'tp', split_axis=0, concat_axis=...  23.2 us
    all_gather x1, blocking collectives, shards(): hidden_bf = lax.all_gather(hidden_part_bf[None], 'tp', axis=0, tiled=True)  19.7 us
    all_to_all x1, waiting for transfers between devices, shards(): lax.all_to_all(attn_blocks.transpose(1, 0, 2), 'tp', split_axis=0, concat...  15.9 us
    reshape x2, local copies, waits for them, and re-layouts, shards(): partial_value.astype(jnp.bfloat16).reshape(-1, tp_count, part_width)  15.2 us
  transfers between devices with their start and end apart: 12, of which 9 were waited for; matrix products, arithmetic and copies ran while one was open for 31% of the time, Pallas kernels for 0%

profile of v1, /device:TPU:2, one launch (start us, length us, event | category | flops | bytes accessed | tf_op | source)
XLA Modules:
  0.0 507.5 jit_solution(17513931402715952241)
XLA Ops:
  17.7 5.0 all-to-all-start
  23.1 4.5 reduce-window.6
  31.1 15.9 %all-to-all-done = bf16[4,192,640]{2,1,0:T(8,128)(2,1)S(1)} async-done(((bf16[4,192,640]{2,1,0:T(8,128)(2,1)}), bf16[4,192,640]{2,1,0:T(8,128)(2,1)S(1)}, u32[]{:S(2)}, u32[]{:S(2)}) %all-to-all-start) | async-done | bytes 983072 | tf_op jit(solution)/shard_map/all_to_all | solution.py:133
  48.2 19.7 %all-gather = bf16[768,640]{1,0:T(8,128)(2,1)S(1)} all-gather(bf16[192,640]{1,0:T(8,128)(2,1)S(1)} %add_convert_fusion.1), channel_id=2, replica_groups=mesh['req'=8,'tp'=4] {'tp'}, dimensions={0}, use_global_device_ids=true | all-gather | bytes 1228800 | tf_op jit(solution)/shard_map/all_gather | solution.py:139
  78.6 4.9 all-to-all-start.4
  85.9 27.8 %all-to-all-done.4 = bf16[8,96,1600]{2,1,0:T(8,128)(2,1)} async-done(((bf16[8,96,1600]{2,1,0:T(8,128)(2,1)}), bf16[8,96,1600]{2,1,0:T(8,128)(2,1)}, u32[]{:S(2)}, u32[]{:S(2)}) %all-to-all-start.4) | async-done | bytes 2457632 | tf_op jit(solution)/shard_map/all_to_all | solution.py:159
  113.7 6.1 %all-to-all-start.1 = ((bf16[8,96,1600]{2,1,0:T(8,128)(2,1)}), bf16[8,96,1600]{2,1,0:T(8,128)(2,1)}, u32[]{:S(2)}, u32[]{:S(2)}) async-start(bf16[8,96,1600]{2,1,0:T(8,128)(2,1)} %convolution_convert_fusion.4), calls=%async_computation.1 | async-start | bytes 5111808 | tf_op jit(solution)/shard_map/all_to_all | solution.py:159
  121.6 13.0 %collective-permute-done.2 = bf16[1,768,320]{1,2,0:T(8,128)(2,1)} collective-permute-done((bf16[1,768,320]{1,2,0:T(8,128)(2,1)S(1)}, bf16[1,768,320]{1,2,0:T(8,128)(2,1)}, u32[]{:S(2)}, u32[]{:S(2)}) %collective-permute-start.2) | collective-permute-done | bytes 491552 | tf_op jit(solution)/shard_map/ppermute | solution.py:19
  140.9 7.6 %fusion.93 = (bf16[1,2560,2,384]{3,2,1,0:T(2,128)(2,1)}, bf16[1,2560,2,384]{3,2,1,0:T(2,128)(2,1)S(1)}) fusion(bf16[2,2560,2,384]{3,2,1,0:T(2,128)(2,1)} %param.30), kind=kLoop, calls=%fused_computation.159 | loop fusion | bytes 15728640 | tf_op jit(solution)/shard_map/slice | solution.py:163
  155.6 5.2 %fusion.27 = f32[768,2,384]{2,0,1:T(8,128)} fusion(bf16[1280,2,384]{2,0,1:T(8,128)(2,1)} %bitcast.248, bf16[768,1600]{1,0:T(8,128)(2,1)} %bitcast.53), kind=kOutput, calls=%fused_computation.49 | convolution fusion | flops 1509949440 | bytes 6291456 | tf_op jit(solution)/shard_map/mk,kcf->mcf/dot_general | solution.py:166
  160.8 24.0 %collective-permute-done.3 = bf16[2,768,320]{1,2,0:T(8,128)(2,1)} collective-permute-done((bf16[2,768,320]{1,2,0:T(8,128)(2,1)}, bf16[2,768,320]{1,2,0:T(8,128)(2,1)}, u32[]{:S(2)}, u32[]{:S(2)}) %collective-permute-start.3) | collective-permute-done | bytes 983072 | tf_op jit(solution)/shard_map/ppermute | solution.py:19
  187.3 5.8 %bitcast_add_fusion = f32[768,2,384]{2,0,1:T(8,128)S(1)} fusion(f32[768,2,384]{2,0,1:T(8,128)} %fusion.27, bf16[4,640,2,384]{3,1,0,2:T(8,128)(2,1)} %bitcast.236, bf16[2,768,320]{2,1,0:T(8,128)(2,1)} %copy.211, bf16[2,768,320]{2,1,0:T(8,128)(2,1)} %maximum_select_fusion.3, pred[]{:T(512)S(6)} %eq.109), kind=kOutput, calls=%fused_computation.43 | convolution fusion | flops 1519386624 | bytes 9043969 | tf_op jit(solution)/shard_map/zmk,zkcf->mcf/dot_general | solution.py:168
  197.3 7.6 %reshape.247 = bf16[768,4,640]{2,1,0:T(4,128)(2,1)} reshape(bf16[768,2560]{1,0:T(8,128)(2,1)} %convolution_convert_fusion) | data formatting | bytes 7864320 | tf_op jit(solution)/shard_map/reshape | solution.py:171
  204.9 7.4 %fusion.95 = (bf16[768,4,320]{2,1,0:T(4,128)(2,1)}, bf16[768,4,320]{2,1,0:T(4,128)(2,1)}) fusion(bf16[768,4,640]{2,1,0:T(4,128)(2,1)} %reshape.247), kind=kLoop, calls=%fused_computation.161 | loop fusion | bytes 7864320 | tf_op jit(solution)/shard_map/slice | solution.py:172
  212.3 5.4 %copy.232 = bf16[768,4,320]{0,2,1:T(8,128)(2,1)} copy(bf16[768,4,320]{2,1,0:T(4,128)(2,1)} %get-tuple-element.10) | data formatting | bytes 3932160
  217.7 4.9 all-to-all-start.5
  233.3 5.9 %fusion.29 = f32[768,2,384]{2,0,1:T(8,128)} fusion(bf16[1280,2,384]{2,0,1:T(8,128)(2,1)S(1)} %bitcast.249, bf16[768,1600]{1,0:T(8,128)(2,1)} %bitcast.36), kind=kOutput, calls=%fused_computation.52 | convolution fusion | flops 1509949440 | bytes 6291456 | tf_op jit(solution)/shard_map/mk,kcf->mcf/dot_general | solution.py:166
  239.2 71.3 %collective-permute-done.1 = bf16[2,768,320]{1,2,0:T(8,128)(2,1)} collective-permute-done((bf16[2,768,320]{1,2,0:T(8,128)(2,1)}, bf16[2,768,320]{1,2,0:T(8,128)(2,1)}, u32[]{:S(2)}, u32[]{:S(2)}) %collective-permute-start.1) | collective-permute-done | bytes 983072 | tf_op jit(solution)/shard_map/ppermute | solution.py:19
  312.9 5.1 %bitcast_add_fusion.1 = f32[768,2,384]{2,0,1:T(8,128)S(1)} fusion(f32[768,2,384]{2,0,1:T(8,128)} %fusion.29, bf16[4,640,2,384]{3,1,0,2:T(8,128)(2,1)} %bitcast.238, bf16[2,768,320]{2,1,0:T(8,128)(2,1)} %copy.199, bf16[2,768,320]{2,1,0:T(8,128)(2,1)S(1)} %copy-done.7, pred[]{:T(512)S(6)} %eq.109), kind=kOutput, calls=%fused_computation.44 | convolution fusion | flops 1519386624 | bytes 8847361 | tf_op jit(solution)/shard_map/zmk,zkcf->mcf/dot_general | solution.py:168
  322.1 7.6 %reshape.244 = bf16[768,4,640]{2,1,0:T(4,128)(2,1)} reshape(bf16[768,2560]{1,0:T(8,128)(2,1)} %convolution_convert_fusion.1) | data formatting | bytes 7864320 | tf_op jit(solution)/shard_map/reshape | solution.py:171
  329.7 7.3 %fusion.94 = (bf16[768,4,320]{2,1,0:T(4,128)(2,1)}, bf16[768,4,320]{2,1,0:T(4,128)(2,1)}) fusion(bf16[768,4,640]{2,1,0:T(4,128)(2,1)} %reshape.244), kind=kLoop, calls=%fused_computation.160 | loop fusion | bytes 7864320 | tf_op jit(solution)/shard_map/slice | solution.py:172
  337.0 5.3 %copy.230 = bf16[768,4,320]{0,2,1:T(8,128)(2,1)} copy(bf16[768,4,320]{2,1,0:T(4,128)(2,1)} %get-tuple-element.8) | data formatting | bytes 3932160
  342.3 4.4 all-to-all-start.2
  346.8 4.7 concatenate.62
  357.1 34.7 %all-to-all-done.2 = bf16[4,768,320]{1,2,0:T(8,128)(2,1)} async-done(((bf16[4,768,320]{1,2,0:T(8,128)(2,1)}), bf16[4,768,320]{1,2,0:T(8,128)(2,1)}, u32[]{:S(2)}, u32[]{:S(2)}) %all-to-all-start.2) | async-done | bytes 1966112 | tf_op jit(solution)/shard_map/all_to_all | solution.py:173
  391.8 5.1 %all-to-all-start.6 = ((bf16[8,96,1600]{2,1,0:T(8,128)(2,1)}), bf16[8,96,1600]{2,1,0:T(8,128)(2,1)}, u32[]{:S(2)}, u32[]{:S(2)}) async-start(bf16[8,96,1600]{2,1,0:T(8,128)(2,1)} %pad_maximum_fusion.1), calls=%async_computation.6 | async-start | bytes 5111808 | tf_op jit(solution)/shard_map/all_to_all | solution.py:182
  405.0 4.7 concatenate.55
  415.3 11.8 %all-to-all-done.6 = bf16[8,96,1600]{2,1,0:T(8,128)(2,1)} async-done(((bf16[8,96,1600]{2,1,0:T(8,128)(2,1)}), bf16[8,96,1600]{2,1,0:T(8,128)(2,1)}, u32[]{:S(2)}, u32[]{:S(2)}) %all-to-all-start.6) | async-done | bytes 2457632 | tf_op jit(solution)/shard_map/all_to_all | solution.py:182
  427.1 5.8 %all-to-all-start.3 = ((bf16[8,96,1600]{2,1,0:T(8,128)(2,1)}), bf16[8,96,1600]{2,1,0:T(8,128)(2,1)}, u32[]{:S(2)}, u32[]{:S(2)}) async-start(bf16[8,96,1600]{2,1,0:T(8,128)(2,1)} %pad_maximum_fusion), calls=%async_computation.3 | async-start | bytes 5111808 | tf_op jit(solution)/shard_map/all_to_all | solution.py:182
  450.2 12.9 %all-to-all-done.3 = bf16[8,96,1600]{2,1,0:T(8,128)(2,1)} async-done(((bf16[8,96,1600]{2,1,0:T(8,128)(2,1)}), bf16[8,96,1600]{2,1,0:T(8,128)(2,1)}, u32[]{:S(2)}, u32[]{:S(2)}) %all-to-all-start.3) | async-done | bytes 2457632 | tf_op jit(solution)/shard_map/all_to_all | solution.py:182
  474.8 4.4 all-to-all-start.7
  480.9 23.2 %all-to-all-done.7 = bf16[4,192,640]{2,1,0:T(8,128)(2,1)} async-done(((bf16[4,192,640]{2,1,0:T(8,128)(2,1)}), bf16[4,192,640]{2,1,0:T(8,128)(2,1)}, u32[]{:S(2)}, u32[]{:S(2)}) %all-to-all-start.7) | async-done | bytes 983072 | tf_op jit(solution)/shard_map/all_to_all | solution.py:212
  (162 shorter events, 127.5 us)
Async XLA Ops:
  0.0 15.7 %copy-start = (bf16[640,2560]{1,0:T(8,128)(2,1)S(1)}, bf16[640,2560]{1,0:T(8,128)(2,1)}, u32[]{:S(2)}) copy-start(bf16[640,2560]{1,0:T(8,128)(2,1)} %param.26) | copy-start | bytes 9830404
  0.0 7.7 %copy-start.17 = (bf16[192,640]{1,0:T(8,128)(2,1)S(1)}, bf16[192,640]{1,0:T(8,128)(2,1)}, u32[]{:S(2)}) copy-start(bf16[192,640]{1,0:T(8,128)(2,1)} %param.17) | copy-start | bytes 737284
  1.8 6.9 %copy-start.26 = (s32[4,48]{1,0:T(4,128)S(1)}, s32[4,48]{1,0:T(4,128)}, u32[]{:S(2)}) copy-start(s32[4,48]{1,0:T(4,128)} %param.24) | copy-start | bytes 2308
  16.6 6.1 %copy-start.21 = (s32[192,6]{0,1:T(8,128)S(1)}, s32[192,6]{0,1:T(8,128)}, u32[]{:S(2)}) copy-start(s32[192,6]{0,1:T(8,128)} %param.29) | copy-start | bytes 13828
  17.7 13.4 %copy-start.20 = (f32[2560]{0:T(1024)S(1)}, f32[2560]{0:T(1024)}, u32[]{:S(2)}) copy-start(f32[2560]{0:T(1024)} %param.27) | copy-start | bytes 30724
  17.7 29.3 %all-to-all-start = ((bf16[4,192,640]{2,1,0:T(8,128)(2,1)}), bf16[4,192,640]{2,1,0:T(8,128)(2,1)S(1)}, u32[]{:S(2)}, u32[]{:S(2)}) async-start(bf16[4,192,640]{2,1,0:T(8,128)(2,1)} %bitcast.228), calls=%async_computation | async-start | bytes 1966080 | tf_op jit(solution)/shard_map/all_to_all | solution.py:133
  78.6 5.0 copy-start.12
  78.6 35.1 %all-to-all-start.4 = ((bf16[8,96,1600]{2,1,0:T(8,128)(2,1)}), bf16[8,96,1600]{2,1,0:T(8,128)(2,1)}, u32[]{:S(2)}, u32[]{:S(2)}) async-start(bf16[8,96,1600]{2,1,0:T(8,128)(2,1)} %convolution_convert_fusion.3), calls=%async_computation.4 | async-start | bytes 5111808 | tf_op jit(solution)/shard_map/all_to_all | solution.py:159
  113.7 38.7 %all-to-all-start.1 = ((bf16[8,96,1600]{2,1,0:T(8,128)(2,1)}), bf16[8,96,1600]{2,1,0:T(8,128)(2,1)}, u32[]{:S(2)}, u32[]{:S(2)}) async-start(bf16[8,96,1600]{2,1,0:T(8,128)(2,1)} %convolution_convert_fusion.4), calls=%async_computation.1 | async-start | bytes 5111808 | tf_op jit(solution)/shard_map/all_to_all | solution.py:159
  121.2 13.4 %collective-permute-start.2 = (bf16[1,768,320]{1,2,0:T(8,128)(2,1)S(1)}, bf16[1,768,320]{1,2,0:T(8,128)(2,1)}, u32[]{:S(2)}, u32[]{:S(2)}) collective-permute-start(bf16[1,768,320]{1,2,0:T(8,128)(2,1)S(1)} %copy.207), channel_id=1, source_target_pairs={{0,1},{1,0},{2,3},{3,2},{4,5},{5,4},{6,7},{7,6},{8,9},{9,8},{10,11... | collective-permute-start | bytes 1474568 | tf_op jit(solution)/shard_map/ppermute | solution.py:19
  139.6 45.2 %collective-permute-start.3 = (bf16[2,768,320]{1,2,0:T(8,128)(2,1)}, bf16[2,768,320]{1,2,0:T(8,128)(2,1)}, u32[]{:S(2)}, u32[]{:S(2)}) collective-permute-start(bf16[2,768,320]{1,2,0:T(8,128)(2,1)} %copy.210), channel_id=1, source_target_pairs={{0,2},{1,3},{2,0},{3,1},{4,6},{5,7},{6,4},{7,5},{8,10},{9,11},{10,... | collective-permute-start | bytes 2949128 | tf_op jit(solution)/shard_map/ppermute | solution.py:19
  153.8 68.7 %collective-permute-start = (bf16[1,768,320]{1,2,0:T(8,128)(2,1)S(1)}, bf16[1,768,320]{1,2,0:T(8,128)(2,1)}, u32[]{:S(2)}, u32[]{:S(2)}) collective-permute-start(bf16[1,768,320]{1,2,0:T(8,128)(2,1)S(1)} %copy.195), channel_id=1, source_target_pairs={{0,1},{1,0},{2,3},{3,2},{4,5},{5,4},{6,7},{7,6},{8,9},{9,8},{10,11... | collective-permute-start | bytes 1474568 | tf_op jit(solution)/shard_map/ppermute | solution.py:19
  187.3 5.8 %copy-start.23 = (bf16[2,384,2560]{2,1,0:T(8,128)(2,1)S(1)}, bf16[2,384,2560]{2,1,0:T(8,128)(2,1)}, u32[]{:S(2)}) copy-start(bf16[2,384,2560]{2,1,0:T(8,128)(2,1)} %param.31) | copy-start | bytes 11796484
  217.7 124.7 %all-to-all-start.5 = ((bf16[4,768,320]{1,2,0:T(8,128)(2,1)}), bf16[4,768,320]{1,2,0:T(8,128)(2,1)}, u32[]{:S(2)}, u32[]{:S(2)}) async-start(bf16[4,768,320]{1,2,0:T(8,128)(2,1)} %bitcast.239), calls=%async_computation.5 | async-start | bytes 3932160 | tf_op jit(solution)/shard_map/all_to_all | solution.py:173
  227.6 82.9 %collective-permute-start.1 = (bf16[2,768,320]{1,2,0:T(8,128)(2,1)}, bf16[2,768,320]{1,2,0:T(8,128)(2,1)}, u32[]{:S(2)}, u32[]{:S(2)}) collective-permute-start(bf16[2,768,320]{1,2,0:T(8,128)(2,1)} %copy.198), channel_id=1, source_target_pairs={{0,2},{1,3},{2,0},{3,1},{4,6},{5,7},{6,4},{7,5},{8,10},{9,11},{10,... | collective-permute-start | bytes 2949128 | tf_op jit(solution)/shard_map/ppermute | solution.py:19
  233.1 6.1 %copy-start.3 = (bf16[1,2560,2,384]{3,1,2,0:T(8,128)(2,1)}, bf16[1,2560,2,384]{3,1,2,0:T(8,128)(2,1)S(1)}, u32[]{:S(2)}) copy-start(bf16[1,2560,2,384]{3,1,2,0:T(8,128)(2,1)S(1)} %copy.194) | copy-start | bytes 11796484
  233.3 79.5 %copy-start.7 = (bf16[2,768,320]{2,1,0:T(8,128)(2,1)S(1)}, bf16[2,768,320]{2,1,0:T(8,128)(2,1)}, u32[]{:S(2)}) copy-start(bf16[2,768,320]{2,1,0:T(8,128)(2,1)} %maximum_select_fusion.2) | copy-start | bytes 2949124
  312.9 5.1 %copy-start.24 = (bf16[2,384,2560]{2,1,0:T(8,128)(2,1)S(1)}, bf16[2,384,2560]{2,1,0:T(8,128)(2,1)}, u32[]{:S(2)}) copy-start(bf16[2,384,2560]{2,1,0:T(8,128)(2,1)} %param.31) | copy-start | bytes 11796484
  342.3 49.5 %all-to-all-start.2 = ((bf16[4,768,320]{1,2,0:T(8,128)(2,1)}), bf16[4,768,320]{1,2,0:T(8,128)(2,1)}, u32[]{:S(2)}, u32[]{:S(2)}) async-start(bf16[4,768,320]{1,2,0:T(8,128)(2,1)} %bitcast.241), calls=%async_computation.2 | async-start | bytes 3932160 | tf_op jit(solution)/shard_map/all_to_all | solution.py:173
  391.8 35.3 %all-to-all-start.6 = ((bf16[8,96,1600]{2,1,0:T(8,128)(2,1)}), bf16[8,96,1600]{2,1,0:T(8,128)(2,1)}, u32[]{:S(2)}, u32[]{:S(2)}) async-start(bf16[8,96,1600]{2,1,0:T(8,128)(2,1)} %pad_maximum_fusion.1), calls=%async_computation.6 | async-start | bytes 5111808 | tf_op jit(solution)/shard_map/all_to_all | solution.py:182
  396.9 4.2 copy-start.13
  415.3 17.6 %copy-start.19 = (f32[192,2,384]{2,0,1:T(8,128)S(1)}, f32[192,2,384]{2,0,1:T(8,128)}, u32[]{:S(2)}) copy-start(f32[192,2,384]{2,0,1:T(8,128)} %fusion.2) | copy-start | bytes 1769476
  427.1 36.0 %all-to-all-start.3 = ((bf16[8,96,1600]{2,1,0:T(8,128)(2,1)}), bf16[8,96,1600]{2,1,0:T(8,128)(2,1)}, u32[]{:S(2)}, u32[]{:S(2)}) async-start(bf16[8,96,1600]{2,1,0:T(8,128)(2,1)} %pad_maximum_fusion), calls=%async_computation.3 | async-start | bytes 5111808 | tf_op jit(solution)/shard_map/all_to_all | solution.py:182
  432.9 3.8 copy-start.18
  435.3 3.2 copy-start.4
  442.6 4.1 copy-start.10
  450.2 15.5 %copy-start.11 = (bf16[192,8,2,96]{3,0,1,2:T(8,128)(2,1)S(1)}, bf16[192,8,2,96]{3,0,1,2:T(8,128)(2,1)}, u32[]{:S(2)}) copy-start(bf16[192,8,2,96]{3,0,1,2:T(8,128)(2,1)} %copy-done.10) | copy-start | bytes 1769476
  463.1 2.6 copy-start.14
  463.1 2.7 copy-start.15
  469.4 3.1 copy-start.5
  473.5 33.8 %copy-start.1 = (bf16[640,2560]{1,0:T(8,128)(2,1)S(1)}, bf16[640,2560]{1,0:T(8,128)(2,1)}, u32[]{:S(2)}) copy-start(bf16[640,2560]{1,0:T(8,128)(2,1)} %param.26) | copy-start | bytes 9830404
  474.8 29.3 %all-to-all-start.7 = ((bf16[4,192,640]{2,1,0:T(8,128)(2,1)}), bf16[4,192,640]{2,1,0:T(8,128)(2,1)}, u32[]{:S(2)}, u32[]{:S(2)}) async-start(bf16[4,192,640]{2,1,0:T(8,128)(2,1)} %maximum_bitcast_fusion), calls=%async_computation.7 | async-start | bytes 1966080 | tf_op jit(solution)/shard_map/all_to_all | solution.py:212
  (7 other events, 10.8 us)
